TPU v7x, 512 devices: a whole 4x8x8 slice. The times are simulated.
512 devices in a mesh: box: 64 (over x, y, z_hi), row: 8 (over z_lo, core).
Axes of the slice: x: 4, y: 8, z: 8 (z_hi: 2, z_lo: 4; z = z_hi * 4 + z_lo), core: 2. Of those that a mesh axis runs over, the one named last changes fastest.
Arguments:
- leaf_maps: float32 [64, 2048, 2048], P('box', 'row'), as said below
- iface_index: int32 [64, 512], replicated, may hold values from 0 to 511, as said below
Outputs:
- merged_maps: bfloat16 [64, 2048, 3072], P('box', 'row')
Inputs may be any that keep to these rules, and one draw needn't show every extreme that they name: Each row of iface_index is a permutation of 0 .. 511. Each leaf_maps[c] is exactly symmetric.
All inputs are finite; a program needn't handle non-finite values.
Results may differ from a plain program's by a relative error of at most 0.001.
Values sent between devices are 32-bit elements; how exact they have to be, the bound alone decides.
No kernel may reach another device: no remote copies, remote signals or barrier semaphores. Data moves between devices by JAX's collectives and lax.ppermute only.
A program may use at most 64 MiB of HBM per device.

v0:
```python
import jax
import jax.numpy as jnp
from jax import lax
from jax.sharding import PartitionSpec as P


def swapped(value, axis, stride):
    mask = 2**stride
    pairs = [(source, source ^ mask) for source in range(lax.axis_size(axis))]
    return lax.ppermute(value, axis, pairs)


def body(leaf_maps, iface_index):
    local = leaf_maps[0]
    rows_here = local.shape[0]
    width = local.shape[1]
    inner = iface_index.shape[1]
    outer = width - inner
    box_id = lax.axis_index("box")
    is_first = box_id % 2 == 0
    partner_id = box_id + 1 - 2 * (box_id % 2)
    own_index = lax.dynamic_index_in_dim(iface_index, box_id, 0, keepdims=False)
    partner_index = lax.dynamic_index_in_dim(iface_index, partner_id, 0, keepdims=False)
    mine = jnp.take(local[:, outer:], own_index, axis=1)
    own_full = lax.all_gather(mine, "row", axis=0, tiled=True)
    other_full = swapped(own_full, "box", 0)
    schur = jnp.take(own_full[outer:], own_index, axis=0) + jnp.take(
        other_full[outer:], partner_index, axis=0
    )
    squared = jnp.dot(schur, schur, precision=lax.Precision.HIGHEST)
    factor = jnp.linalg.cholesky(squared)
    first_ext = jnp.where(is_first, own_full[:outer], other_full[:outer])
    second_ext = jnp.where(is_first, other_full[:outer], own_full[:outer])
    global_rows = lax.axis_index("row") * rows_here + jnp.arange(rows_here, dtype=jnp.int32)
    unit = (own_index[None, :] == (global_rows - outer)[:, None]).astype(jnp.float32)
    replaced = jnp.logical_and(is_first, global_rows >= outer)
    left = jnp.where(replaced[:, None], unit, mine)
    local_ext = local[:, :outer]
    zero = jnp.zeros((), jnp.float32)
    left_part = jnp.where(jnp.logical_and(is_first, global_rows < outer)[:, None], local_ext, zero)
    right_part = jnp.where(is_first, zero, local_ext)
    base = jnp.concatenate([left_part, right_part], 1)
    turned = jnp.dot(schur, left.T, precision=lax.Precision.HIGHEST)
    solved = jax.scipy.linalg.cho_solve((factor, True), turned).T
    contract = (((1,), (1,)), ((), ()))
    update_first = lax.dot_general(solved, first_ext, contract, precision=lax.Precision.HIGHEST)
    update_second = lax.dot_general(solved, second_ext, contract, precision=lax.Precision.HIGHEST)
    merged = base - jnp.concatenate([update_first, update_second], 1)
    return merged.astype(jnp.bfloat16)[None]


def solution(mesh):
    in_specs = (P("box", "row", None), P())
    out_specs = P("box", "row", None)
    return jax.shard_map(body, mesh=mesh, in_specs=in_specs, out_specs=out_specs, check_vma=False)
```

profile of v0, /device:TPU:4, one launch (start us, length us, event | category | flops | bytes accessed | tf_op | source)
XLA Modules:
  0.0 439.9 jit_solution(11699187846083616787)
XLA Ops:
  6.5 0.7 constant_dynamic-slice_fusion.1
  7.3 0.7 compare_select_fusion
  8.0 1.1 slice.191
  9.3 1.6 gather_fusion
  10.9 1.0 select_bitcast_fusion.2
  11.9 62.4 %all-gather.2.cloned.1.call-done = f32[2048,512]{0,1:T(8,128)} async-done(((f32[256,512]{0,1:T(8,128)}), f32[2048,512]{0,1:T(8,128)}) %all-gather.2.cloned.1.call-update) | async-done | bytes 4194320 | tf_op jit(solution)/shard_map/all_gather | solution.py:25
  74.2 5.3 %collective-permute-start = (f32[2048,512]{0,1:T(8,128)}, f32[2048,512]{0,1:T(8,128)}, u32[]{:S(2)}, u32[]{:S(2)}) collective-permute-start(f32[2048,512]{0,1:T(8,128)} %all-gather.2.cloned.1.call-done), channel_id=1, source_target_pairs={{0,8},{8,0},{16,24},{24,16},{32,40},{40,32},{48,56},{56,48},{64,72... | collective-permute-start | bytes 12582920 | tf_op jit(solution)/shard_map/ppermute | solution.py:10
  79.7 1.9 select_bitcast_fusion.1
  81.5 1.3 slice.192
  83.2 1.6 gather_fusion.1
  84.8 177.5 %collective-permute-done = f32[2048,512]{0,1:T(8,128)} collective-permute-done((f32[2048,512]{0,1:T(8,128)}, f32[2048,512]{0,1:T(8,128)}, u32[]{:S(2)}, u32[]{:S(2)}) %collective-permute-start) | collective-permute-done | bytes 4194336 | tf_op jit(solution)/shard_map/ppermute | solution.py:10
  262.3 1.3 slice.193
  263.9 2.1 gather_fusion.2
  266.0 2.2 fusion.74
  268.2 1.3 copy.10
  269.5 1.4 fusion.17
  271.0 1.0 copy-done.5
  272.0 11.7 %cholesky.104 = f32[128,128]{1,0:T(8,128)S(1)} custom-call(f32[128,128]{1,0:T(8,128)S(1)} %cholesky.266), custom_call_target="Cholesky" | custom-call | tf_op jit(solution)/shard_map/jit(cholesky)/cholesky | solution.py:31
  283.9 9.8 %custom-call.34 = f32[1,128,128]{1,2,0:T(8,128)S(1)} custom-call(f32[1,128,128]{2,1,0:T(8,128)S(1)} %get-tuple-element.37), custom_call_target="InvertDiagBlocksLowerTriangular" | custom-call | tf_op jit(solution)/shard_map/jit(cholesky)/cholesky | solution.py:31
  293.7 1.2 constant_dynamic-update-slice_fusion.2
  294.9 1.3 convolution_subtract_fusion
  296.2 11.9 %cholesky.217 = f32[128,128]{1,0:T(8,128)S(1)} custom-call(f32[128,128]{1,0:T(8,128)S(1)} %cholesky.270), custom_call_target="Cholesky" | custom-call | tf_op jit(solution)/shard_map/jit(cholesky)/cholesky | solution.py:31
  308.1 0.7 compare_reduce_fusion.2
  308.8 0.7 compare_reduce_fusion.3
  309.4 9.8 %custom-call.35 = f32[1,128,128]{1,2,0:T(8,128)S(1)} custom-call(f32[1,128,128]{2,1,0:T(8,128)S(1)} %get-tuple-element.34), custom_call_target="InvertDiagBlocksLowerTriangular" | custom-call | tf_op jit(solution)/shard_map/jit(cholesky)/cholesky | solution.py:31
  319.5 1.3 convolution_subtract_fusion.5
  320.8 11.7 %cholesky.238 = f32[128,128]{1,0:T(8,128)S(1)} custom-call(f32[128,128]{1,0:T(8,128)S(1)} %cholesky.275), custom_call_target="Cholesky" | custom-call | tf_op jit(solution)/shard_map/jit(cholesky)/cholesky | solution.py:31
  332.6 0.6 compare_reduce_fusion.1
  333.2 9.8 %custom-call.36 = f32[1,128,128]{1,2,0:T(8,128)S(1)} custom-call(f32[1,128,128]{2,1,0:T(8,128)S(1)} %get-tuple-element.31), custom_call_target="InvertDiagBlocksLowerTriangular" | custom-call | tf_op jit(solution)/shard_map/jit(cholesky)/cholesky | solution.py:31
  343.2 1.2 convolution_subtract_fusion.8
  344.5 11.9 %cholesky.255 = f32[128,128]{1,0:T(8,128)S(1)} custom-call(f32[128,128]{1,0:T(8,128)S(1)} %convolution_subtract_fusion.8), custom_call_target="Cholesky" | custom-call | tf_op jit(solution)/shard_map/jit(cholesky)/cholesky | solution.py:31
  356.4 0.6 compare_reduce_fusion
  359.4 1.1 select_select_fusion
  360.6 14.0 %while.1 = (s32[]{:T(128)}, f32[512,512]{1,0:T(8,128)}, s32[4,2]{0,1:T(2,128)S(1)}, f32[4,128,128]{2,1,0:T(8,128)}, s32[]{:T(128)}) while((s32[]{:T(128)}, f32[512,512]{1,0:T(8,128)}, s32[4,2]{0,1:T(2,128)S(1)}, f32[4,128,128]{2,1,0:T(8,128)}, s32[]{:T(128)}) %tuple.31), condition=%wide.while_cond, body=%wide.while_body.sunk | while | flops 2 | bytes 132705 | solution.py:44
  360.6 0.5 fusion.87
  361.2 2.9 bitcast_dynamic-update-slice_fusion.2
  364.1 0.5 fusion.87
  364.7 2.9 bitcast_dynamic-update-slice_fusion.2
  367.6 0.5 fusion.87
  368.2 2.9 bitcast_dynamic-update-slice_fusion.2
  371.1 0.5 fusion.87
  371.7 2.8 bitcast_dynamic-update-slice_fusion.2
  374.5 40.2 %custom-call.37 = f32[4,128,128]{1,2,0:T(8,128)S(1)} custom-call(f32[4,128,128]{2,1,0:T(8,128)} %get-tuple-element.13), custom_call_target="InvertDiagBlocksLowerTriangular" | custom-call | tf_op jit(solution)/shard_map/jit(_cho_solve)/triangular_solve | solution.py:44
  414.7 2.3 fusion.18
  420.8 0.5 convolution_subtract_fusion.1
  421.6 4.8 %fusion.9 = f32[1,256,1536]{2,1,0:T(8,128)S(1)} fusion(f32[2048,512]{0,1:T(8,128)} %collective-permute-done, f32[2048,512]{0,1:T(8,128)S(1)} %copy-done, pred[]{:T(512)S(6)} %eq.19, f32[128,256]{1,0:T(8,128)S(1)} %fusion.65, f32[128,256]{1,0:T(8,128)S(1)} %fusion.63, f32[128,256]{1,0:T(8,128)S(1)} %fusion.61, f32[128,256]{1,0:T(8,128)S(1)} %fusion.60), kind=kOutput, calls=%fused_computation.15 | convolution fusion | flops 2417098752 | bytes 8388609 | tf_op jit(solution)/shard_map/dot_general | solution.py:46
  426.4 4.9 %fusion.12 = f32[1,256,1536]{2,1,0:T(8,128)S(1)} fusion(f32[2048,512]{0,1:T(8,128)} %collective-permute-done, f32[2048,512]{0,1:T(8,128)S(1)} %copy-done, pred[]{:T(512)S(6)} %eq.19, f32[128,256]{1,0:T(8,128)S(1)} %fusion.65, f32[128,256]{1,0:T(8,128)S(1)} %fusion.63, f32[128,256]{1,0:T(8,128)S(1)} %fusion.61, f32[128,256]{1,0:T(8,128)S(1)} %fusion.60), kind=kOutput, calls=%fused_computation.16 | convolution fusion | flops 2417098752 | bytes 8388609 | tf_op jit(solution)/shard_map/dot_general | solution.py:47
  431.3 1.5 fusion
  (56 shorter events, 5.9 us)
Async XLA Ops:
  6.5 67.7 %all-gather.2.cloned.1.call-start = ((), (), s32[]{:S(2)}) async-start(), calls=%async_computation | async-start | bytes 4718592 | tf_op jit(solution)/shard_map/all_gather | solution.py:25
  9.3 70.4 %copy-start.6 = (f32[1,256,2048]{2,1,0:T(8,128)S(1)}, f32[1,256,2048]{2,1,0:T(8,128)}, u32[]{:S(2)}) copy-start(f32[1,256,2048]{2,1,0:T(8,128)} %param.4) | copy-start | bytes 6291460
  10.9 70.7 %copy-start.3 = (f32[512,256]{1,0:T(8,128)}, f32[512,256]{1,0:T(8,128)S(1)}, u32[]{:S(2)}) copy-start(f32[512,256]{1,0:T(8,128)S(1)} %gather_fusion) | copy-start | bytes 1572868
  74.2 188.0 %collective-permute-start = (f32[2048,512]{0,1:T(8,128)}, f32[2048,512]{0,1:T(8,128)}, u32[]{:S(2)}, u32[]{:S(2)}) collective-permute-start(f32[2048,512]{0,1:T(8,128)} %all-gather.2.cloned.1.call-done), channel_id=1, source_target_pairs={{0,8},{8,0},{16,24},{24,16},{32,40},{40,32},{48,56},{56,48},{64,72... | collective-permute-start | bytes 12582920 | tf_op jit(solution)/shard_map/ppermute | solution.py:10
  271.0 1.0 copy-start.5
  374.5 42.8 %copy-start.4 = (f32[512,512]{1,0:T(8,128)S(1)}, f32[512,512]{1,0:T(8,128)}, u32[]{:S(2)}) copy-start(f32[512,512]{1,0:T(8,128)} %get-tuple-element.91) | copy-start | bytes 3145732
  417.3 4.2 copy-start
  426.4 4.9 %copy-start.1 = (f32[1,256,1536]{2,1,0:T(8,128)S(1)}, f32[1,256,1536]{2,1,0:T(8,128)}, u32[]{:S(2)}) copy-start(f32[1,256,1536]{2,1,0:T(8,128)} %get-tuple-element.26) | copy-start | bytes 4718596
  426.4 4.9 %copy-start.2 = (f32[1,256,1536]{2,1,0:T(8,128)S(1)}, f32[1,256,1536]{2,1,0:T(8,128)}, u32[]{:S(2)}) copy-start(f32[1,256,1536]{2,1,0:T(8,128)} %get-tuple-element.27) | copy-start | bytes 4718596
Sparse Core Ops, SparseCore 0:
  12.0 62.1 all-gather.1
where the time goes:
time: 444 us; the launch traced here: 440 us
  waiting for transfers between devices  240 us (54%)
  other arithmetic  127 us (29%)
  local copies, waits for them, and re-layouts  27 us (6%)
  matrix products  24 us (5%)
  between operations  16.5 us (4%)
  starting transfers between devices  5.3 us (1%)
    ppermute x1, waiting for transfers between devices, swapped(): return lax.ppermute(value, axis, pairs)  177 us
    another operation x15, other arithmetic, body(): factor = jnp.linalg.cholesky(squared)  79.3 us
    all_gather x1, waiting for transfers between devices, body(): own_full = lax.all_gather(mine, 'row', axis=0, tiled=True)  62.4 us
    another operation x3, other arithmetic, body(): solved = jax.scipy.linalg.cho_solve((factor, True), turned).T  41.4 us
    another operation x12, local copies, waits for them, and re-layouts  14 us
  transfers between devices with their start and end apart: 2, of which 2 were waited for; matrix products, arithmetic and copies ran while one was open for 1% of the time, Pallas kernels for 0%

commit v1 on v0

--- a/solution.py
+++ b/solution.py
@@ -22,7 +22,11 @@
     own_index = lax.dynamic_index_in_dim(iface_index, box_id, 0, keepdims=False)
     partner_index = lax.dynamic_index_in_dim(iface_index, partner_id, 0, keepdims=False)
     mine = jnp.take(local[:, outer:], own_index, axis=1)
-    own_full = lax.all_gather(mine, "row", axis=0, tiled=True)
+    local_data_reach = lambda u: jnp.concatenate(
+        lax.all_to_all(jnp.stack([u for _ in range(lax.axis_size("row"))], axis=0), "row", 0, 0),
+        axis=0,
+    )
+    own_full = local_data_reach(mine)
     other_full = swapped(own_full, "box", 0)
     schur = jnp.take(own_full[outer:], own_index, axis=0) + jnp.take(
         other_full[outer:], partner_index, axis=0

time: 444 us -> 474 us (1.068)
  the two profiles are of different devices: /device:TPU:4 before, /device:TPU:1 now
where the time goes in v1:
time: 474 us; the launch traced here: 470 us
  waiting for transfers between devices  171 us (36%)
  other arithmetic  129 us (27%)
  blocking collectives  103 us (22%)
  local copies, waits for them, and re-layouts  31.4 us (7%)
  matrix products  25.3 us (5%)
  starting transfers between devices  6.5 us (1%)
    ppermute x1, waiting for transfers between devices, swapped(): return lax.ppermute(value, axis, pairs)  171 us
    all_to_all x1, blocking collectives, body(): lax.all_to_all(jnp.stack([u for _ in range(lax.axis_size('row'))], axis=0...  103 us
    another operation x14, other arithmetic, body(): factor = jnp.linalg.cholesky(squared)  78.8 us
    another operation x3, other arithmetic, body(): solved = jax.scipy.linalg.cho_solve((factor, True), turned).T  41.3 us
    another operation x12, local copies, waits for them, and re-layouts  14.1 us
  transfers between devices with their start and end apart: 1, of which 1 were waited for; matrix products, arithmetic and copies ran while one was open for 2% of the time, Pallas kernels for 0%

profile of v1, /device:TPU:1, one launch (start us, length us, event | category | flops | bytes accessed | tf_op | source)
XLA Modules:
  0.0 470.0 jit_solution(14552358674076919377)
XLA Ops:
  0.0 0.7 compare_select_fusion
  0.7 1.1 slice.199
  2.0 1.6 gather_fusion
  4.0 0.5 stack.2
  4.5 103.2 %all_to_all.5 = f32[8,256,512]{2,1,0:T(8,128)} all-to-all(f32[8,256,512]{2,1,0:T(8,128)S(1)} %stack.2), channel_id=1, replica_groups=mesh['box'=64,'row'=8] {'row'}, dimensions={0} | all-to-all | bytes 8388608 | tf_op jit(solution)/shard_map/all_to_all | solution.py:26
  107.7 6.5 %collective-permute-start = (f32[2048,512]{1,0:T(8,128)}, f32[2048,512]{1,0:T(8,128)}, u32[]{:S(2)}, u32[]{:S(2)}) collective-permute-start(f32[2048,512]{1,0:T(8,128)} %bitcast.9), channel_id=1, source_target_pairs={{0,8},{8,0},{16,24},{24,16},{32,40},{40,32},{48,56},{56,48},{64,72... | collective-permute-start | bytes 12582920 | tf_op jit(solution)/shard_map/ppermute | solution.py:10
  114.3 0.7 constant_dynamic-slice_fusion.1
  115.1 1.9 select_bitcast_fusion.1
  116.9 1.3 slice.200
  118.2 1.6 gather_fusion.1
  119.9 4.2 slice.202
  124.1 171.4 %collective-permute-done = f32[2048,512]{1,0:T(8,128)} collective-permute-done((f32[2048,512]{1,0:T(8,128)}, f32[2048,512]{1,0:T(8,128)}, u32[]{:S(2)}, u32[]{:S(2)}) %collective-permute-start) | collective-permute-done | bytes 4194336 | tf_op jit(solution)/shard_map/ppermute | solution.py:10
  295.5 1.3 slice.201
  296.8 2.1 gather_fusion.2
  299.0 2.2 fusion.58
  301.2 1.3 copy.8
  302.5 1.4 fusion.1
  303.9 1.0 copy-done.5
  304.9 11.7 %cholesky.104 = f32[128,128]{1,0:T(8,128)S(1)} custom-call(f32[128,128]{1,0:T(8,128)S(1)} %cholesky.266), custom_call_target="Cholesky" | custom-call | tf_op jit(solution)/shard_map/jit(cholesky)/cholesky | solution.py:35
  316.8 9.8 %custom-call.34 = f32[1,128,128]{1,2,0:T(8,128)S(1)} custom-call(f32[1,128,128]{2,1,0:T(8,128)S(1)} %get-tuple-element.39), custom_call_target="InvertDiagBlocksLowerTriangular" | custom-call | tf_op jit(solution)/shard_map/jit(cholesky)/cholesky | solution.py:35
  326.6 1.2 constant_dynamic-update-slice_fusion.2
  327.9 1.3 convolution_subtract_fusion
  329.1 11.9 %cholesky.217 = f32[128,128]{1,0:T(8,128)S(1)} custom-call(f32[128,128]{1,0:T(8,128)S(1)} %cholesky.270), custom_call_target="Cholesky" | custom-call | tf_op jit(solution)/shard_map/jit(cholesky)/cholesky | solution.py:35
  341.0 9.8 %custom-call.35 = f32[1,128,128]{1,2,0:T(8,128)S(1)} custom-call(f32[1,128,128]{2,1,0:T(8,128)S(1)} %get-tuple-element.36), custom_call_target="InvertDiagBlocksLowerTriangular" | custom-call | tf_op jit(solution)/shard_map/jit(cholesky)/cholesky | solution.py:35
  351.1 1.3 convolution_subtract_fusion.5
  352.4 11.7 %cholesky.238 = f32[128,128]{1,0:T(8,128)S(1)} custom-call(f32[128,128]{1,0:T(8,128)S(1)} %cholesky.275), custom_call_target="Cholesky" | custom-call | tf_op jit(solution)/shard_map/jit(cholesky)/cholesky | solution.py:35
  364.2 0.7 compare_reduce_fusion.1
  364.8 9.8 %custom-call.36 = f32[1,128,128]{1,2,0:T(8,128)S(1)} custom-call(f32[1,128,128]{2,1,0:T(8,128)S(1)} %get-tuple-element.33), custom_call_target="InvertDiagBlocksLowerTriangular" | custom-call | tf_op jit(solution)/shard_map/jit(cholesky)/cholesky | solution.py:35
  374.9 1.2 convolution_subtract_fusion.8
  376.1 11.9 %cholesky.255 = f32[128,128]{1,0:T(8,128)S(1)} custom-call(f32[128,128]{1,0:T(8,128)S(1)} %convolution_subtract_fusion.8), custom_call_target="Cholesky" | custom-call | tf_op jit(solution)/shard_map/jit(cholesky)/cholesky | solution.py:35
  388.0 0.7 compare_reduce_fusion
  388.7 0.7 compare_reduce_fusion.2
  392.0 1.1 select_select_fusion
  393.1 14.1 %while.1 = (s32[]{:T(128)}, f32[512,512]{1,0:T(8,128)}, s32[4,2]{0,1:T(2,128)S(1)}, f32[4,128,128]{2,1,0:T(8,128)}, s32[]{:T(128)}) while((s32[]{:T(128)}, f32[512,512]{1,0:T(8,128)}, s32[4,2]{0,1:T(2,128)S(1)}, f32[4,128,128]{2,1,0:T(8,128)}, s32[]{:T(128)}) %tuple.31), condition=%wide.while_cond, body=%wide.while_body.sunk | while | flops 2 | bytes 132705 | solution.py:48
  393.1 0.6 fusion.73
  393.7 2.9 bitcast_dynamic-update-slice_fusion.2
  396.7 0.6 fusion.73
  397.3 2.9 bitcast_dynamic-update-slice_fusion.2
  400.2 0.6 fusion.73
  400.8 2.9 bitcast_dynamic-update-slice_fusion.2
  403.8 0.6 fusion.73
  404.3 2.8 bitcast_dynamic-update-slice_fusion.2
  407.2 40.2 %custom-call.37 = f32[4,128,128]{1,2,0:T(8,128)S(1)} custom-call(f32[4,128,128]{2,1,0:T(8,128)} %get-tuple-element.13), custom_call_target="InvertDiagBlocksLowerTriangular" | custom-call | tf_op jit(solution)/shard_map/jit(_cho_solve)/triangular_solve | solution.py:48
  447.4 2.3 fusion.2
  454.2 3.0 bitcast_select_fusion.1
  457.3 5.3 %convolution_bitcast_fusion.1 = f32[1,256,1536]{2,1,0:T(8,128)S(1)} fusion(f32[1536,512]{1,0:T(8,128)S(1)} %get-tuple-element.26, f32[128,256]{1,0:T(8,128)S(1)} %fusion.49, f32[128,256]{1,0:T(8,128)S(1)} %fusion.47, f32[128,256]{1,0:T(8,128)S(1)} %fusion.45, f32[128,256]{1,0:T(8,128)S(1)} %fusion.44), kind=kOutput, calls=%fused_computation.10 | convolution fusion | flops 2416312320 | bytes 5242880 | tf_op jit(solution)/shard_map/dot_general | solution.py:50
  462.7 5.6 %convolution_bitcast_fusion = f32[1,256,1536]{2,1,0:T(8,128)S(1)} fusion(f32[1536,512]{1,0:T(8,128)S(1)} %get-tuple-element.27, f32[128,256]{1,0:T(8,128)S(1)} %fusion.49, f32[128,256]{1,0:T(8,128)S(1)} %fusion.47, f32[128,256]{1,0:T(8,128)S(1)} %fusion.45, f32[128,256]{1,0:T(8,128)S(1)} %fusion.44), kind=kOutput, calls=%fused_computation.9 | convolution fusion | flops 2416312320 | bytes 5242880 | tf_op jit(solution)/shard_map/dot_general | solution.py:51
  468.3 1.5 fusion
  (57 shorter events, 6.1 us)
Async XLA Ops:
  3.6 0.9 copy-start.3
  4.5 110.6 %copy-start.6 = (f32[1,256,2048]{2,1,0:T(8,128)S(1)}, f32[1,256,2048]{2,1,0:T(8,128)}, u32[]{:S(2)}) copy-start(f32[1,256,2048]{2,1,0:T(8,128)} %param.4) | copy-start | bytes 6291460
  107.7 187.9 %collective-permute-start = (f32[2048,512]{1,0:T(8,128)}, f32[2048,512]{1,0:T(8,128)}, u32[]{:S(2)}, u32[]{:S(2)}) collective-permute-start(f32[2048,512]{1,0:T(8,128)} %bitcast.9), channel_id=1, source_target_pairs={{0,8},{8,0},{16,24},{24,16},{32,40},{40,32},{48,56},{56,48},{64,72... | collective-permute-start | bytes 12582920 | tf_op jit(solution)/shard_map/ppermute | solution.py:10
  303.9 1.0 copy-start.5
  407.2 42.8 %copy-start.4 = (f32[512,512]{1,0:T(8,128)S(1)}, f32[512,512]{1,0:T(8,128)}, u32[]{:S(2)}) copy-start(f32[512,512]{1,0:T(8,128)} %get-tuple-element.88) | copy-start | bytes 3145732
  450.0 4.2 copy-start
  462.6 5.6 %copy-start.1 = (f32[1,256,1536]{2,1,0:T(8,128)S(1)}, f32[1,256,1536]{2,1,0:T(8,128)}, u32[]{:S(2)}) copy-start(f32[1,256,1536]{2,1,0:T(8,128)} %get-tuple-element.28) | copy-start | bytes 4718596
  462.6 5.6 %copy-start.2 = (f32[1,256,1536]{2,1,0:T(8,128)S(1)}, f32[1,256,1536]{2,1,0:T(8,128)}, u32[]{:S(2)}) copy-start(f32[1,256,1536]{2,1,0:T(8,128)} %get-tuple-element.29) | copy-start | bytes 4718596
